TPU v7x, 256 devices: a whole 4x4x8 slice. The times are simulated.
256 devices in a mesh: seq: 64 (over z, x, core), head: 4 (over y).
Axes of the slice: x: 4, y: 4, z: 8, core: 2. Of those that a mesh axis runs over, the one named last changes fastest.
Arguments:
- features: bfloat16 [8192, 4096], P('seq', 'head'), may hold values from -6 to 6
- proj_weight: bfloat16 [4096, 4096], P(None, 'head'), may hold values from -0.09375 to 0.09375
- query_vectors: bfloat16 [8192, 4096], P('seq', 'head'), may hold values from -6 to 6
- key_vectors: bfloat16 [8192, 4096], P('seq', 'head'), may hold values from -6 to 6
Outputs:
- rotated_queries: bfloat16 [8192, 4096], P('seq', 'head')
- rotated_keys: bfloat16 [8192, 4096], P('seq', 'head')
All inputs are finite; a program needn't handle non-finite values.
Results may differ from a plain program's by a relative error of at most 0.0024.
Values may be sent and summed in bfloat16 or wider, within the bound.
No kernel may reach another device: no remote copies, remote signals or barrier semaphores. Data moves between devices by JAX's collectives and lax.ppermute only.
A program may use at most 128 MiB of HBM per device.

v0:
```python
import functools
import jax
import jax.numpy as jnp
from jax import lax
from jax.sharding import PartitionSpec as P

HEAD_DIM = 128


def entering(array, axis, count, combine, identity):
    place = lax.axis_index(axis)
    start = jnp.broadcast_to(jnp.asarray(identity, array.dtype), array.shape)
    span = array
    before = None
    shift = 1
    while shift < count:
        pairs = [(k, k + shift) for k in range(count - shift)]
        arrived = lax.ppermute(span, axis, pairs)
        reached = place >= shift
        last = shift * 2 >= count
        if before is None:
            before = jnp.where(reached, arrived, start)
            if not last:
                span = jnp.where(reached, combine(arrived, span), span)
        elif last:
            before = jnp.where(reached, combine(arrived, before), before)
        else:
            width = array.shape[-1]
            both = combine(arrived, jnp.concatenate([span, before], axis=-1))
            span = jnp.where(reached, both[..., :width], span)
            before = jnp.where(reached, both[..., width:], before)
        shift = shift * 2
    return before if before is not None else start


def small_inverse(matrix):
    highest = lax.Precision.HIGHEST
    size = matrix.shape[-1]
    position = jnp.arange(size)
    strict = (position[:, None] < position[None, :]).astype(jnp.float32)
    eye_block = jnp.eye(size, dtype=jnp.float32)
    power = -2.0 * matrix * strict[None]
    result = eye_block[None] + power
    reach = 2
    while reach < size:
        power = jnp.einsum("hij,hjk->hik", power, power, precision=highest)
        result = result + jnp.einsum("hij,hjk->hik", result, power, precision=highest)
        reach = reach * 2
    return 2.0 * result


def triangle_inverse(matrix):
    highest = lax.Precision.HIGHEST
    size = matrix.shape[-1]
    if size <= 16:
        return small_inverse(matrix)
    half = size // 2
    first = triangle_inverse(matrix[:, :half, :half])
    second = triangle_inverse(matrix[:, half:, half:])
    coupling = matrix[:, :half, half:]
    middle = jnp.einsum("hij,hjk->hik", first, coupling, precision=highest)
    corner = -jnp.einsum("hij,hjk->hik", middle, second, precision=highest)
    lower_left = jnp.zeros((matrix.shape[0], size - half, half), jnp.float32)
    top = jnp.concatenate([first, corner], axis=2)
    bottom = jnp.concatenate([lower_left, second], axis=2)
    return jnp.concatenate([top, bottom], axis=1)


def upper_solve(matrix, right_side):
    highest = lax.Precision.HIGHEST
    rows = matrix.shape[1]
    size = min(128, rows)
    count = rows // size
    solved_blocks = []
    for i in reversed(range(count)):
        inverse_block = triangle_inverse(matrix)
        solved_blocks.append(
            jnp.einsum("hij,hjk->hik", inverse_block, right_side, precision=highest)
        )
    return jnp.concatenate(solved_blocks[::-1], axis=1)


def body(seq_count, features, proj_weight, query_vectors, key_vectors):
    highest = lax.Precision.HIGHEST
    tok_rows = query_vectors.shape[0]
    width = proj_weight.shape[1]
    local_heads = width // HEAD_DIM
    raw_proj = jnp.dot(
        lax.all_gather(features, "head", axis=1, tiled=True),
        proj_weight,
        preferred_element_type=jnp.float32,
    )
    raw_proj = raw_proj.reshape(tok_rows, local_heads, HEAD_DIM)
    directions = raw_proj * lax.rsqrt(jnp.sum(raw_proj * raw_proj, axis=-1, keepdims=True) + 1e-06)
    reflectors = jnp.transpose(directions, (1, 0, 2))
    targets = jnp.concatenate(
        [
            query_vectors.reshape(tok_rows, local_heads, HEAD_DIM),
            key_vectors.reshape(tok_rows, local_heads, HEAD_DIM),
        ],
        axis=0,
    )
    targets = jnp.transpose(targets.astype(jnp.float32), (1, 0, 2))
    gram = jnp.einsum("hid,hjd->hij", reflectors, reflectors, precision=highest)
    position = jnp.arange(tok_rows)
    upper = (position[:, None] < position[None, :]).astype(jnp.float32)
    identity_tok = jnp.eye(tok_rows, dtype=jnp.float32)
    inverse_t = gram * upper[None] + 0.5 * identity_tok[None]
    projected = jnp.einsum("hid,htd->hit", reflectors, targets, precision=highest)
    target_pos = jnp.concatenate([position, position])
    keep = (position[:, None] <= target_pos[None, :]).astype(jnp.float32)
    masked = projected * keep[None]
    right_side = jnp.concatenate([masked, reflectors], axis=2)
    solved = upper_solve(inverse_t, right_side)
    weights_tok = solved[:, :, : 2 * tok_rows]
    factor = solved[:, :, 2 * tok_rows :]
    local_part = targets - jnp.einsum("hit,hid->htd", weights_tok, reflectors, precision=highest)
    identity = jnp.broadcast_to(
        jnp.eye(HEAD_DIM, dtype=jnp.float32), (local_heads, HEAD_DIM, HEAD_DIM)
    )
    block_product = identity - jnp.einsum("hid,hie->hde", reflectors, factor, precision=highest)

    def combine(earlier, later):
        return jnp.einsum("hde,hef->hdf", earlier, later, precision=highest)

    carried = entering(block_product, "seq", seq_count, combine, identity)
    rotated = jnp.einsum("hde,hte->htd", carried, local_part, precision=highest)
    rotated = jnp.transpose(rotated, (1, 0, 2))
    rotated_queries = rotated[:tok_rows].reshape(tok_rows, width).astype(jnp.bfloat16)
    rotated_keys = rotated[tok_rows:].reshape(tok_rows, width).astype(jnp.bfloat16)
    return (rotated_queries, rotated_keys)


def solution(mesh):
    in_specs = (P("seq", "head"), P(None, "head"), P("seq", "head"), P("seq", "head"))
    out_specs = (P("seq", "head"), P("seq", "head"))
    return jax.shard_map(
        functools.partial(body, mesh.shape["seq"]),
        mesh=mesh,
        in_specs=in_specs,
        out_specs=out_specs,
        check_vma=False,
    )
```

profile of v0, /device:TPU:35, one launch (start us, length us, event | category | flops | bytes accessed | tf_op | source)
XLA Modules:
  0.0 207.6 jit_solution(11913831428166195170)
XLA Ops:
  7.2 0.7 all-gather.2.cloned.1.call-update
  7.9 1.1 copy.86
  9.2 1.1 copy.85
  10.8 26.2 %all-gather.2.cloned.1.call-done = bf16[128,4096]{1,0:T(8,128)(2,1)} async-done(((bf16[128,1024]{1,0:T(8,128)(2,1)}), bf16[128,4096]{1,0:T(8,128)(2,1)}) %all-gather.2.cloned.1.call-update) | async-done | bytes 1048592 | tf_op jit(solution)/shard_map/all_gather | solution.py:89
  37.0 5.0 %fusion.141 = f32[128,1024]{1,0:T(8,128)S(1)} fusion(bf16[128,4096]{1,0:T(8,128)(2,1)} %all-gather.2.cloned.1.call-done, bf16[4096,1024]{1,0:T(8,128)(2,1)} %param.5), kind=kOutput, calls=%fused_computation.212 | convolution fusion | flops 1073741824 | bytes 9961472 | tf_op jit(solution)/shard_map/dot_general | solution.py:88
  42.6 1.2 fusion.5
  59.5 1.7 fusion
  61.2 1.0 convolution_subtract_fusion.1
  62.2 5.7 %collective-permute-start = (f32[8,128,128]{1,2,0:T(8,128)S(1)}, f32[8,128,128]{1,2,0:T(8,128)S(1)}, u32[]{:S(2)}, u32[]{:S(2)}) collective-permute-start(f32[8,128,128]{1,2,0:T(8,128)S(1)} %convolution_subtract_fusion.1), channel_id=1, source_target_pairs={{0,4},{4,8},{8,12},{12,16},{16,20},{20,24},{24,28},{28,32},{32,36}... | collective-permute-start | bytes 1572872 | tf_op jit(solution)/shard_map/ppermute | solution.py:18
  68.0 6.1 %collective-permute-done = f32[8,128,128]{1,2,0:T(8,128)S(1)} collective-permute-done((f32[8,128,128]{1,2,0:T(8,128)S(1)}, f32[8,128,128]{1,2,0:T(8,128)S(1)}, u32[]{:S(2)}, u32[]{:S(2)}) %collective-permute-start) | collective-permute-done | bytes 524320 | tf_op jit(solution)/shard_map/ppermute | solution.py:18
  74.1 1.8 convolution_select_fusion.1
  75.9 2.8 %collective-permute-start.1 = (f32[8,128,128]{1,2,0:T(8,128)S(1)}, f32[8,128,128]{1,2,0:T(8,128)}, u32[]{:S(2)}, u32[]{:S(2)}) collective-permute-start(f32[8,128,128]{1,2,0:T(8,128)S(1)} %convolution_select_fusion.1), channel_id=1, source_target_pairs={{0,8},{4,12},{8,16},{12,20},{16,24},{20,28},{24,32},{28,36},{32,40... | collective-permute-start | bytes 1572872 | tf_op jit(solution)/shard_map/ppermute | solution.py:18
  78.7 10.6 %collective-permute-done.1 = f32[8,128,128]{1,2,0:T(8,128)} collective-permute-done((f32[8,128,128]{1,2,0:T(8,128)S(1)}, f32[8,128,128]{1,2,0:T(8,128)}, u32[]{:S(2)}, u32[]{:S(2)}) %collective-permute-start.1) | collective-permute-done | bytes 524320 | tf_op jit(solution)/shard_map/ppermute | solution.py:18
  89.3 2.0 fusion.15
  91.3 1.1 slice_select_fusion.7
  92.5 4.6 %collective-permute-start.2 = (f32[8,128,128]{1,2,0:T(8,128)}, f32[8,128,128]{1,2,0:T(8,128)S(1)}, u32[]{:S(2)}, u32[]{:S(2)}) collective-permute-start(f32[8,128,128]{1,2,0:T(8,128)} %get-tuple-element.15), channel_id=1, source_target_pairs={{0,16},{4,20},{8,24},{12,28},{16,32},{20,36},{24,40},{28,44},{32,4... | collective-permute-start | bytes 1572872 | tf_op jit(solution)/shard_map/ppermute | solution.py:18
  97.1 10.6 %collective-permute-done.2 = f32[8,128,128]{1,2,0:T(8,128)S(1)} collective-permute-done((f32[8,128,128]{1,2,0:T(8,128)}, f32[8,128,128]{1,2,0:T(8,128)S(1)}, u32[]{:S(2)}, u32[]{:S(2)}) %collective-permute-start.2) | collective-permute-done | bytes 524320 | tf_op jit(solution)/shard_map/ppermute | solution.py:18
  107.7 2.2 %fusion.19 = f32[8,128,256]{1,2,0:T(8,128)S(1)} fusion(f32[8,128,128]{1,2,0:T(8,128)S(1)} %collective-permute-done.2, f32[8,128,128]{1,2,0:T(8,128)} %get-tuple-element.14, f32[8,128,128]{1,2,0:T(8,128)} %get-tuple-element.15), kind=kOutput, calls=%fused_computation.57 | convolution fusion | flops 402915328 | bytes 2621440 | tf_op jit(solution)/shard_map/hde,hef->hdf/dot_general | solution.py:124
  109.9 0.9 slice_select_fusion.5
  110.8 3.2 %collective-permute-start.3 = (f32[8,128,128]{1,2,0:T(8,128)}, f32[8,128,128]{1,2,0:T(8,128)S(1)}, u32[]{:S(2)}, u32[]{:S(2)}) collective-permute-start(f32[8,128,128]{1,2,0:T(8,128)} %get-tuple-element.13), channel_id=1, source_target_pairs={{0,32},{4,36},{8,40},{12,44},{16,48},{20,52},{24,56},{28,60},{32,6... | collective-permute-start | bytes 1572872 | tf_op jit(solution)/shard_map/ppermute | solution.py:18
  114.0 8.6 %collective-permute-done.3 = f32[8,128,128]{1,2,0:T(8,128)S(1)} collective-permute-done((f32[8,128,128]{1,2,0:T(8,128)}, f32[8,128,128]{1,2,0:T(8,128)S(1)}, u32[]{:S(2)}, u32[]{:S(2)}) %collective-permute-start.3) | collective-permute-done | bytes 524320 | tf_op jit(solution)/shard_map/ppermute | solution.py:18
  122.6 2.0 fusion.23
  124.8 9.3 %collective-permute-start.4 = (f32[8,128,128]{1,2,0:T(8,128)S(1)}, f32[8,128,128]{1,2,0:T(8,128)}, u32[]{:S(2)}, u32[]{:S(2)}) collective-permute-start(f32[8,128,128]{1,2,0:T(8,128)S(1)} %get-tuple-element.11), channel_id=1, source_target_pairs={{0,64},{4,68},{8,72},{12,76},{16,80},{20,84},{24,88},{28,92},{32,9... | collective-permute-start | bytes 1572872 | tf_op jit(solution)/shard_map/ppermute | solution.py:18
  134.1 32.4 %collective-permute-done.4 = f32[8,128,128]{1,2,0:T(8,128)} collective-permute-done((f32[8,128,128]{1,2,0:T(8,128)S(1)}, f32[8,128,128]{1,2,0:T(8,128)}, u32[]{:S(2)}, u32[]{:S(2)}) %collective-permute-start.4) | collective-permute-done | bytes 524320 | tf_op jit(solution)/shard_map/ppermute | solution.py:18
  166.6 2.0 fusion.27
  168.6 1.0 slice_select_fusion.2
  169.8 6.0 %collective-permute-start.5 = (f32[8,128,128]{1,2,0:T(8,128)}, f32[8,128,128]{1,2,0:T(8,128)S(1)}, u32[]{:S(2)}, u32[]{:S(2)}) collective-permute-start(f32[8,128,128]{1,2,0:T(8,128)} %slice_select_fusion.2), channel_id=1, source_target_pairs={{0,128},{4,132},{8,136},{12,140},{16,144},{20,148},{24,152},{28,15... | collective-permute-start | bytes 1572872 | tf_op jit(solution)/shard_map/ppermute | solution.py:18
  175.8 3.0 %convolution_subtract_fusion = f32[8,256,128]{2,1,0:T(8,128)S(1)} fusion(f32[8,128,128]{2,1,0:T(8,128)S(1)} %fusion.31, f32[8,128,384]{2,1,0:T(8,128)S(1)} %fusion, bf16[128,8,128]{2,0,1:T(8,128)(2,1)S(1)} %copy.88, bf16[128,8,128]{2,0,1:T(8,128)(2,1)} %copy-done.4), kind=kOutput, calls=%fused_computation.4 | convolution fusion | flops 404226048 | bytes 3145728 | tf_op jit(solution)/shard_map/hit,hid->htd/dot_general | solution.py:117
  178.8 18.4 %collective-permute-done.5 = f32[8,128,128]{1,2,0:T(8,128)S(1)} collective-permute-done((f32[8,128,128]{1,2,0:T(8,128)}, f32[8,128,128]{1,2,0:T(8,128)S(1)}, u32[]{:S(2)}, u32[]{:S(2)}) %collective-permute-start.5) | collective-permute-done | bytes 524320 | tf_op jit(solution)/shard_map/ppermute | solution.py:18
  197.8 1.1 fusion.4
  199.0 0.9 copy.115
  199.9 0.8 copy.116
  (102 shorter events, 17.5 us)
Async XLA Ops:
  7.2 29.8 %all-gather.2.cloned.1.call-start = ((), (), s32[]{:S(2)}) async-start(), calls=%async_computation | async-start | bytes 1310720 | tf_op jit(solution)/shard_map/all_gather | solution.py:89
  10.5 48.3 %copy-start.4 = (bf16[128,8,128]{2,0,1:T(8,128)(2,1)}, bf16[128,8,128]{2,0,1:T(8,128)(2,1)S(1)}, u32[]{:S(2)}) copy-start(bf16[128,8,128]{2,0,1:T(8,128)(2,1)S(1)} %copy.87) | copy-start | bytes 786436
  62.2 5.8 %copy-start.5 = (f32[8,128,128]{1,2,0:T(8,128)}, f32[8,128,128]{1,2,0:T(8,128)S(1)}, u32[]{:S(2)}) copy-start(f32[8,128,128]{1,2,0:T(8,128)S(1)} %convolution_subtract_fusion.1) | copy-start | bytes 1572868
  62.2 11.9 %collective-permute-start = (f32[8,128,128]{1,2,0:T(8,128)S(1)}, f32[8,128,128]{1,2,0:T(8,128)S(1)}, u32[]{:S(2)}, u32[]{:S(2)}) collective-permute-start(f32[8,128,128]{1,2,0:T(8,128)S(1)} %convolution_subtract_fusion.1), channel_id=1, source_target_pairs={{0,4},{4,8},{8,12},{12,16},{16,20},{20,24},{24,28},{28,32},{32,36}... | collective-permute-start | bytes 1572872 | tf_op jit(solution)/shard_map/ppermute | solution.py:18
  75.9 13.4 %collective-permute-start.1 = (f32[8,128,128]{1,2,0:T(8,128)S(1)}, f32[8,128,128]{1,2,0:T(8,128)}, u32[]{:S(2)}, u32[]{:S(2)}) collective-permute-start(f32[8,128,128]{1,2,0:T(8,128)S(1)} %convolution_select_fusion.1), channel_id=1, source_target_pairs={{0,8},{4,12},{8,16},{12,20},{16,24},{20,28},{24,32},{28,36},{32,40... | collective-permute-start | bytes 1572872 | tf_op jit(solution)/shard_map/ppermute | solution.py:18
  92.5 17.4 %copy-start = (f32[8,128,128]{1,2,0:T(8,128)S(1)}, f32[8,128,128]{1,2,0:T(8,128)}, u32[]{:S(2)}) copy-start(f32[8,128,128]{1,2,0:T(8,128)} %get-tuple-element.14) | copy-start | bytes 1572868
  92.5 15.2 %collective-permute-start.2 = (f32[8,128,128]{1,2,0:T(8,128)}, f32[8,128,128]{1,2,0:T(8,128)S(1)}, u32[]{:S(2)}, u32[]{:S(2)}) collective-permute-start(f32[8,128,128]{1,2,0:T(8,128)} %get-tuple-element.15), channel_id=1, source_target_pairs={{0,16},{4,20},{8,24},{12,28},{16,32},{20,36},{24,40},{28,44},{32,4... | collective-permute-start | bytes 1572872 | tf_op jit(solution)/shard_map/ppermute | solution.py:18
  110.8 11.8 %copy-start.1 = (f32[8,128,128]{1,2,0:T(8,128)}, f32[8,128,128]{1,2,0:T(8,128)S(1)}, u32[]{:S(2)}) copy-start(f32[8,128,128]{1,2,0:T(8,128)S(1)} %get-tuple-element.12) | copy-start | bytes 1572868
  110.8 11.8 %collective-permute-start.3 = (f32[8,128,128]{1,2,0:T(8,128)}, f32[8,128,128]{1,2,0:T(8,128)S(1)}, u32[]{:S(2)}, u32[]{:S(2)}) collective-permute-start(f32[8,128,128]{1,2,0:T(8,128)} %get-tuple-element.13), channel_id=1, source_target_pairs={{0,32},{4,36},{8,40},{12,44},{16,48},{20,52},{24,56},{28,60},{32,6... | collective-permute-start | bytes 1572872 | tf_op jit(solution)/shard_map/ppermute | solution.py:18
  124.8 41.8 %collective-permute-start.4 = (f32[8,128,128]{1,2,0:T(8,128)S(1)}, f32[8,128,128]{1,2,0:T(8,128)}, u32[]{:S(2)}, u32[]{:S(2)}) collective-permute-start(f32[8,128,128]{1,2,0:T(8,128)S(1)} %get-tuple-element.11), channel_id=1, source_target_pairs={{0,64},{4,68},{8,72},{12,76},{16,80},{20,84},{24,88},{28,92},{32,9... | collective-permute-start | bytes 1572872 | tf_op jit(solution)/shard_map/ppermute | solution.py:18
  168.6 1.2 copy-start.2
  169.8 27.4 %collective-permute-start.5 = (f32[8,128,128]{1,2,0:T(8,128)}, f32[8,128,128]{1,2,0:T(8,128)S(1)}, u32[]{:S(2)}, u32[]{:S(2)}) collective-permute-start(f32[8,128,128]{1,2,0:T(8,128)} %slice_select_fusion.2), channel_id=1, source_target_pairs={{0,128},{4,132},{8,136},{12,140},{16,144},{20,148},{24,152},{28,15... | collective-permute-start | bytes 1572872 | tf_op jit(solution)/shard_map/ppermute | solution.py:18
  175.8 21.4 %copy-start.3 = (f32[8,128,256]{1,2,0:T(8,128)S(1)}, f32[8,128,256]{1,2,0:T(8,128)}, u32[]{:S(2)}) copy-start(f32[8,128,256]{1,2,0:T(8,128)} %copy-done.2) | copy-start | bytes 3145732
Sparse Core Ops, SparseCore 0:
  9.8 27.1 all-gather.1
where the time goes:
time: 208 us
  waiting for transfers between devices  114 us (55%)
  matrix products  38.3 us (18%)
  starting transfers between devices  31.7 us (15%)
  between operations  14.8 us (7%)
  local copies, waits for them, and re-layouts  5.15 us (2%)
  other arithmetic  4.06 us (2%)
    ppermute x6, waiting for transfers between devices, entering(): arrived = lax.ppermute(span, axis, pairs)  86.6 us
    ppermute x6, starting transfers between devices, entering(): arrived = lax.ppermute(span, axis, pairs)  31.7 us
    all_gather x1, waiting for transfers between devices, body(): lax.all_gather(features, 'head', axis=1, tiled=True)  26.2 us
    dot_general x6, matrix products, combine(): return jnp.einsum('hde,hef->hdf', earlier, later, precision=highest)  10.7 us
    dot_general x24, matrix products, small_inverse(): power = jnp.einsum('hij,hjk->hik', power, power, precision=highest)  5.09 us
    dot_general x24, matrix products, small_inverse(): jnp.einsum('hij,hjk->hik', result, power, precision=highest)  5.05 us
    dot_general x1, matrix products, body(): jnp.dot(lax.all_gather(features, 'head', axis=1, tiled=True), proj_weight...  4.97 us
    unnamed x17, local copies, waits for them, and re-layouts  4.26 us
  transfers between devices with their start and end apart: 7, of which 7 were waited for; matrix products, arithmetic and copies ran while one was open for 3% of the time, Pallas kernels for 0%

commit v1 on v0

--- a/solution.py
+++ b/solution.py
@@ -86,7 +86,9 @@
     width = proj_weight.shape[1]
     local_heads = width // HEAD_DIM
     raw_proj = jnp.dot(
-        lax.all_gather(features, "head", axis=1, tiled=True),
+        jnp.concatenate(
+            lax.all_to_all(jnp.stack([features] * lax.axis_size("head")), "head", 0, 0), axis=1
+        ),
         proj_weight,
         preferred_element_type=jnp.float32,
     )

time: 208 us -> 190 us (0.913)
  waiting for transfers between devices: 114 us -> 86.7 us
  local copies, waits for them, and re-layouts: 5.15 us -> 18.7 us
  between operations: 14.8 us -> 1.47 us
  starting transfers between devices: 31.7 us -> 38.1 us
    all_gather x1 -> x0, waiting for transfers between devices: 26.2 us -> none  [body(): lax.all_gather(features, 'head', axis=1, tiled=True)]
    dot_general x0 -> x1, local copies, waits for them, and re-layouts: none -> 11.3 us  [body(): jnp.dot(jnp.concatenate(lax.all_to_all(jnp.stack([features] * lax.axis_si...]
    all_to_all x0 -> x1, starting transfers between devices: none -> 4.18 us  [body(): lax.all_to_all(jnp.stack([features] * lax.axis_size('head')), 'head', 0, 0)]
    unnamed x17 -> x26, local copies, waits for them, and re-layouts: 4.26 us -> 1.98 us
    ppermute x6, starting transfers between devices: 31.7 us -> 33.9 us  [entering(): arrived = lax.ppermute(span, axis, pairs)]
    another operation x0 -> x1, local copies, waits for them, and re-layouts: none -> 2.17 us  [body(): jnp.stack([features] * lax.axis_size('head'))]
  transfers between devices with their start and end apart: 7 -> 7, of which waited for: 7 -> 7; matrix products, arithmetic and copies ran while one was open for 3% -> 8% of each run, Pallas kernels for 0% -> 0%
where the time goes in v1:
time: 190 us; the launch traced here: 189 us
  waiting for transfers between devices  86.7 us (46%)
  matrix products  39 us (21%)
  starting transfers between devices  38.1 us (20%)
  local copies, waits for them, and re-layouts  18.7 us (10%)
  other arithmetic  4.89 us (3%)
    ppermute x6, waiting for transfers between devices, entering(): arrived = lax.ppermute(span, axis, pairs)  85.4 us
    ppermute x6, starting transfers between devices, entering(): arrived = lax.ppermute(span, axis, pairs)  33.9 us
    dot_general x1, local copies, waits for them, and re-layouts, body(): jnp.dot(jnp.concatenate(lax.all_to_all(jnp.stack([features] * lax.axis_si...  11.3 us
    dot_general x6, matrix products, combine(): return jnp.einsum('hde,hef->hdf', earlier, later, precision=highest)  10.8 us
    dot_general x1, matrix products, body(): jnp.dot(jnp.concatenate(lax.all_to_all(jnp.stack([features] * lax.axis_si...  5.72 us
    dot_general x24, matrix products, small_inverse(): power = jnp.einsum('hij,hjk->hik', power, power, precision=highest)  5.09 us
    dot_general x24, matrix products, small_inverse(): jnp.einsum('hij,hjk->hik', result, power, precision=highest)  5.04 us
    all_to_all x1, starting transfers between devices, body(): lax.all_to_all(jnp.stack([features] * lax.axis_size('head')), 'head', 0, 0)  4.18 us
  transfers between devices with their start and end apart: 7, of which 7 were waited for; matrix products, arithmetic and copies ran while one was open for 8% of the time, Pallas kernels for 0%

profile of v1, /device:TPU:35, one launch (start us, length us, event | category | flops | bytes accessed | tf_op | source)
XLA Modules:
  0.0 188.8 jit_solution(4118693638022314917)
XLA Ops:
  0.6 2.2 %stack.2 = bf16[4,128,1024]{2,1,0:T(8,128)(2,1)} broadcast(bf16[128,1024]{1,0:T(8,128)(2,1)} %param.4), dimensions={1,2} | broadcast | bytes 1310720 | tf_op jit(solution)/shard_map/stack | solution.py:90
  2.8 4.2 %all-to-all-start = ((bf16[4,128,1024]{2,1,0:T(8,128)(2,1)}), bf16[4,128,1024]{2,1,0:T(8,128)(2,1)S(1)}, u32[]{:S(2)}, u32[]{:S(2)}) async-start(bf16[4,128,1024]{2,1,0:T(8,128)(2,1)} %stack.2), calls=%async_computation | async-start | bytes 2097152 | tf_op jit(solution)/shard_map/all_to_all | solution.py:90
  7.0 11.3 %copy.83 = bf16[1024,4096]{1,0:T(8,128)(2,1)} copy(bf16[1024,4096]{0,1:T(8,128)(2,1)} %bitcast.133) | data formatting | bytes 16777216 | tf_op jit(solution)/shard_map/dot_general | solution.py:88
  19.9 1.3 all-to-all-done
  22.9 5.7 %multiply_reduce_fusion = (f32[128,8]{0,1:T(8,128)S(1)}, f32[128,8,128]{0,2,1:T(8,128)S(1)}) fusion(bf16[128,4096,1]{1,0,2:T(8,128)(2,1)S(1)} %reshape.99, bf16[8,128,4096]{2,1,0:T(8,128)(2,1)} %bitcast.132), kind=kOutput, calls=%fused_computation.94 | convolution fusion | flops 1074002944 | bytes 9965568 | tf_op jit(solution)/shard_map/dot_general | solution.py:88
  28.7 1.0 copy.41
  29.7 1.0 fusion.5
  46.5 1.7 fusion
  48.2 1.0 convolution_subtract_fusion.1
  49.2 4.8 %collective-permute-start = (f32[8,128,128]{1,2,0:T(8,128)S(1)}, f32[8,128,128]{1,2,0:T(8,128)S(1)}, u32[]{:S(2)}, u32[]{:S(2)}) collective-permute-start(f32[8,128,128]{1,2,0:T(8,128)S(1)} %convolution_subtract_fusion.1), channel_id=1, source_target_pairs={{0,4},{4,8},{8,12},{12,16},{16,20},{20,24},{24,28},{28,32},{32,36}... | collective-permute-start | bytes 1572872 | tf_op jit(solution)/shard_map/ppermute | solution.py:18
  54.1 6.1 %collective-permute-done = f32[8,128,128]{1,2,0:T(8,128)S(1)} collective-permute-done((f32[8,128,128]{1,2,0:T(8,128)S(1)}, f32[8,128,128]{1,2,0:T(8,128)S(1)}, u32[]{:S(2)}, u32[]{:S(2)}) %collective-permute-start) | collective-permute-done | bytes 524320 | tf_op jit(solution)/shard_map/ppermute | solution.py:18
  60.2 1.9 convolution_select_fusion.1
  62.0 2.8 %collective-permute-start.1 = (f32[8,128,128]{1,2,0:T(8,128)S(1)}, f32[8,128,128]{1,2,0:T(8,128)}, u32[]{:S(2)}, u32[]{:S(2)}) collective-permute-start(f32[8,128,128]{1,2,0:T(8,128)S(1)} %convolution_select_fusion.1), channel_id=1, source_target_pairs={{0,8},{4,12},{8,16},{12,20},{16,24},{20,28},{24,32},{28,36},{32,40... | collective-permute-start | bytes 1572872 | tf_op jit(solution)/shard_map/ppermute | solution.py:18
  64.9 10.6 %collective-permute-done.1 = f32[8,128,128]{1,2,0:T(8,128)} collective-permute-done((f32[8,128,128]{1,2,0:T(8,128)S(1)}, f32[8,128,128]{1,2,0:T(8,128)}, u32[]{:S(2)}, u32[]{:S(2)}) %collective-permute-start.1) | collective-permute-done | bytes 524320 | tf_op jit(solution)/shard_map/ppermute | solution.py:18
  75.5 2.0 %fusion.15 = f32[8,128,256]{1,2,0:T(8,128)S(1)} fusion(f32[8,128,128]{1,2,0:T(8,128)} %collective-permute-done.1, f32[8,128,128]{1,2,0:T(8,128)S(1)} %broadcast_select_fusion, f32[8,128,128]{1,2,0:T(8,128)S(1)} %convolution_select_fusion.1), kind=kOutput, calls=%fused_computation.53 | convolution fusion | flops 402915328 | bytes 2621440 | tf_op jit(solution)/shard_map/hde,hef->hdf/dot_general | solution.py:126
  77.5 1.1 slice_select_fusion.7
  78.7 5.2 %collective-permute-start.2 = (f32[8,128,128]{1,2,0:T(8,128)}, f32[8,128,128]{1,2,0:T(8,128)S(1)}, u32[]{:S(2)}, u32[]{:S(2)}) collective-permute-start(f32[8,128,128]{1,2,0:T(8,128)} %get-tuple-element.11), channel_id=1, source_target_pairs={{0,16},{4,20},{8,24},{12,28},{16,32},{20,36},{24,40},{28,44},{32,4... | collective-permute-start | bytes 1572872 | tf_op jit(solution)/shard_map/ppermute | solution.py:18
  83.9 10.0 %collective-permute-done.2 = f32[8,128,128]{1,2,0:T(8,128)S(1)} collective-permute-done((f32[8,128,128]{1,2,0:T(8,128)}, f32[8,128,128]{1,2,0:T(8,128)S(1)}, u32[]{:S(2)}, u32[]{:S(2)}) %collective-permute-start.2) | collective-permute-done | bytes 524320 | tf_op jit(solution)/shard_map/ppermute | solution.py:18
  93.9 2.2 %fusion.19 = f32[8,128,256]{1,2,0:T(8,128)S(1)} fusion(f32[8,128,128]{1,2,0:T(8,128)S(1)} %collective-permute-done.2, f32[8,128,128]{1,2,0:T(8,128)} %get-tuple-element.10, f32[8,128,128]{1,2,0:T(8,128)} %get-tuple-element.11), kind=kOutput, calls=%fused_computation.57 | convolution fusion | flops 402915328 | bytes 2621440 | tf_op jit(solution)/shard_map/hde,hef->hdf/dot_general | solution.py:126
  96.1 0.9 slice_select_fusion.5
  97.0 3.5 %collective-permute-start.3 = (f32[8,128,128]{1,2,0:T(8,128)}, f32[8,128,128]{1,2,0:T(8,128)S(1)}, u32[]{:S(2)}, u32[]{:S(2)}) collective-permute-start(f32[8,128,128]{1,2,0:T(8,128)} %get-tuple-element.9), channel_id=1, source_target_pairs={{0,32},{4,36},{8,40},{12,44},{16,48},{20,52},{24,56},{28,60},{32,6... | collective-permute-start | bytes 1572872 | tf_op jit(solution)/shard_map/ppermute | solution.py:18
  100.6 8.3 %collective-permute-done.3 = f32[8,128,128]{1,2,0:T(8,128)S(1)} collective-permute-done((f32[8,128,128]{1,2,0:T(8,128)}, f32[8,128,128]{1,2,0:T(8,128)S(1)}, u32[]{:S(2)}, u32[]{:S(2)}) %collective-permute-start.3) | collective-permute-done | bytes 524320 | tf_op jit(solution)/shard_map/ppermute | solution.py:18
  108.9 2.0 %fusion.23 = f32[8,128,256]{1,2,0:T(8,128)S(1)} fusion(f32[8,128,128]{1,2,0:T(8,128)S(1)} %collective-permute-done.3, f32[8,128,128]{1,2,0:T(8,128)S(1)} %get-tuple-element.8, f32[8,128,128]{1,2,0:T(8,128)} %get-tuple-element.9), kind=kOutput, calls=%fused_computation.61 | convolution fusion | flops 402915328 | bytes 2621440 | tf_op jit(solution)/shard_map/hde,hef->hdf/dot_general | solution.py:126
  111.1 11.2 %collective-permute-start.4 = (f32[8,128,128]{1,2,0:T(8,128)S(1)}, f32[8,128,128]{1,2,0:T(8,128)}, u32[]{:S(2)}, u32[]{:S(2)}) collective-permute-start(f32[8,128,128]{1,2,0:T(8,128)S(1)} %get-tuple-element.7), channel_id=1, source_target_pairs={{0,64},{4,68},{8,72},{12,76},{16,80},{20,84},{24,88},{28,92},{32,9... | collective-permute-start | bytes 1572872 | tf_op jit(solution)/shard_map/ppermute | solution.py:18
  122.2 32.4 %collective-permute-done.4 = f32[8,128,128]{1,2,0:T(8,128)} collective-permute-done((f32[8,128,128]{1,2,0:T(8,128)S(1)}, f32[8,128,128]{1,2,0:T(8,128)}, u32[]{:S(2)}, u32[]{:S(2)}) %collective-permute-start.4) | collective-permute-done | bytes 524320 | tf_op jit(solution)/shard_map/ppermute | solution.py:18
  154.7 2.0 %fusion.27 = f32[8,128,256]{1,2,0:T(8,128)S(1)} fusion(f32[8,128,128]{1,2,0:T(8,128)} %collective-permute-done.4, f32[8,128,128]{1,2,0:T(8,128)S(1)} %get-tuple-element.6, f32[8,128,128]{1,2,0:T(8,128)S(1)} %get-tuple-element.7), kind=kOutput, calls=%fused_computation.65 | convolution fusion | flops 402915328 | bytes 2621440 | tf_op jit(solution)/shard_map/hde,hef->hdf/dot_general | solution.py:126
  156.7 0.9 slice_select_fusion.2
  157.9 6.3 %collective-permute-start.5 = (f32[8,128,128]{1,2,0:T(8,128)}, f32[8,128,128]{1,2,0:T(8,128)S(1)}, u32[]{:S(2)}, u32[]{:S(2)}) collective-permute-start(f32[8,128,128]{1,2,0:T(8,128)} %slice_select_fusion.2), channel_id=1, source_target_pairs={{0,128},{4,132},{8,136},{12,140},{16,144},{20,148},{24,152},{28,15... | collective-permute-start | bytes 1572872 | tf_op jit(solution)/shard_map/ppermute | solution.py:18
  164.2 3.1 %convolution_subtract_fusion = f32[8,256,128]{2,1,0:T(8,128)S(1)} fusion(f32[8,128,128]{1,2,0:T(8,128)S(1)} %bitcast_multiply_fusion, f32[8,128,384]{2,1,0:T(8,128)S(1)} %fusion, bf16[128,8,128]{2,0,1:T(8,128)(2,1)} %copy-done.5, bf16[128,8,128]{2,0,1:T(8,128)(2,1)} %copy-done.6), kind=kOutput, calls=%fused_computation.4 | convolution fusion | flops 404226048 | bytes 3145728 | tf_op jit(solution)/shard_map/hit,hid->htd/dot_general | solution.py:119
  167.3 18.0 %collective-permute-done.5 = f32[8,128,128]{1,2,0:T(8,128)S(1)} collective-permute-done((f32[8,128,128]{1,2,0:T(8,128)}, f32[8,128,128]{1,2,0:T(8,128)S(1)}, u32[]{:S(2)}, u32[]{:S(2)}) %collective-permute-start.5) | collective-permute-done | bytes 524320 | tf_op jit(solution)/shard_map/ppermute | solution.py:18
  185.9 1.1 fusion.4
  187.1 0.9 copy.63
  (112 shorter events, 20.5 us)
Async XLA Ops:
  0.6 19.1 %copy-start = (bf16[128,1024]{1,0:T(8,128)(2,1)S(1)}, bf16[128,1024]{1,0:T(8,128)(2,1)}, u32[]{:S(2)}) copy-start(bf16[128,1024]{1,0:T(8,128)(2,1)} %param.6) | copy-start | bytes 786436
  2.8 18.4 %all-to-all-start = ((bf16[4,128,1024]{2,1,0:T(8,128)(2,1)}), bf16[4,128,1024]{2,1,0:T(8,128)(2,1)S(1)}, u32[]{:S(2)}, u32[]{:S(2)}) async-start(bf16[4,128,1024]{2,1,0:T(8,128)(2,1)} %stack.2), calls=%async_computation | async-start | bytes 2097152 | tf_op jit(solution)/shard_map/all_to_all | solution.py:90
  7.0 12.7 %copy-start.10 = (bf16[128,1024]{1,0:T(8,128)(2,1)S(1)}, bf16[128,1024]{1,0:T(8,128)(2,1)}, u32[]{:S(2)}) copy-start(bf16[128,1024]{1,0:T(8,128)(2,1)} %param.7) | copy-start | bytes 786436
  19.9 25.9 %copy-start.5 = (bf16[128,8,128]{2,0,1:T(8,128)(2,1)}, bf16[128,8,128]{2,0,1:T(8,128)(2,1)S(1)}, u32[]{:S(2)}) copy-start(bf16[128,8,128]{2,0,1:T(8,128)(2,1)S(1)} %get-tuple-element.16) | copy-start | bytes 786436
  19.9 25.9 %copy-start.6 = (bf16[128,8,128]{2,0,1:T(8,128)(2,1)}, bf16[128,8,128]{2,0,1:T(8,128)(2,1)S(1)}, u32[]{:S(2)}) copy-start(bf16[128,8,128]{2,0,1:T(8,128)(2,1)S(1)} %get-tuple-element.17) | copy-start | bytes 786436
  28.6 1.1 copy-start.11
  43.6 2.2 %copy-start.9 = (f32[128,256]{1,0:T(8,128)S(1)}, f32[128,256]{1,0:T(8,128)}, u32[]{:S(2)}) copy-start(f32[128,256]{1,0:T(8,128)} %fusion.74) | copy-start | bytes 393220
  45.4 1.1 copy-start.8
  49.2 4.8 %copy-start.7 = (f32[8,128,128]{1,2,0:T(8,128)}, f32[8,128,128]{1,2,0:T(8,128)S(1)}, u32[]{:S(2)}) copy-start(f32[8,128,128]{1,2,0:T(8,128)S(1)} %convolution_subtract_fusion.1) | copy-start | bytes 1572868
  49.2 10.9 %collective-permute-start = (f32[8,128,128]{1,2,0:T(8,128)S(1)}, f32[8,128,128]{1,2,0:T(8,128)S(1)}, u32[]{:S(2)}, u32[]{:S(2)}) collective-permute-start(f32[8,128,128]{1,2,0:T(8,128)S(1)} %convolution_subtract_fusion.1), channel_id=1, source_target_pairs={{0,4},{4,8},{8,12},{12,16},{16,20},{20,24},{24,28},{28,32},{32,36}... | collective-permute-start | bytes 1572872 | tf_op jit(solution)/shard_map/ppermute | solution.py:18
  62.0 13.5 %collective-permute-start.1 = (f32[8,128,128]{1,2,0:T(8,128)S(1)}, f32[8,128,128]{1,2,0:T(8,128)}, u32[]{:S(2)}, u32[]{:S(2)}) collective-permute-start(f32[8,128,128]{1,2,0:T(8,128)S(1)} %convolution_select_fusion.1), channel_id=1, source_target_pairs={{0,8},{4,12},{8,16},{12,20},{16,24},{20,28},{24,32},{28,36},{32,40... | collective-permute-start | bytes 1572872 | tf_op jit(solution)/shard_map/ppermute | solution.py:18
  78.7 17.4 %copy-start.1 = (f32[8,128,128]{1,2,0:T(8,128)S(1)}, f32[8,128,128]{1,2,0:T(8,128)}, u32[]{:S(2)}) copy-start(f32[8,128,128]{1,2,0:T(8,128)} %get-tuple-element.10) | copy-start | bytes 1572868
  78.7 15.2 %collective-permute-start.2 = (f32[8,128,128]{1,2,0:T(8,128)}, f32[8,128,128]{1,2,0:T(8,128)S(1)}, u32[]{:S(2)}, u32[]{:S(2)}) collective-permute-start(f32[8,128,128]{1,2,0:T(8,128)} %get-tuple-element.11), channel_id=1, source_target_pairs={{0,16},{4,20},{8,24},{12,28},{16,32},{20,36},{24,40},{28,44},{32,4... | collective-permute-start | bytes 1572872 | tf_op jit(solution)/shard_map/ppermute | solution.py:18
  97.0 11.8 %copy-start.2 = (f32[8,128,128]{1,2,0:T(8,128)}, f32[8,128,128]{1,2,0:T(8,128)S(1)}, u32[]{:S(2)}) copy-start(f32[8,128,128]{1,2,0:T(8,128)S(1)} %get-tuple-element.8) | copy-start | bytes 1572868
  97.0 11.8 %collective-permute-start.3 = (f32[8,128,128]{1,2,0:T(8,128)}, f32[8,128,128]{1,2,0:T(8,128)S(1)}, u32[]{:S(2)}, u32[]{:S(2)}) collective-permute-start(f32[8,128,128]{1,2,0:T(8,128)} %get-tuple-element.9), channel_id=1, source_target_pairs={{0,32},{4,36},{8,40},{12,44},{16,48},{20,52},{24,56},{28,60},{32,6... | collective-permute-start | bytes 1572872 | tf_op jit(solution)/shard_map/ppermute | solution.py:18
  111.1 43.6 %collective-permute-start.4 = (f32[8,128,128]{1,2,0:T(8,128)S(1)}, f32[8,128,128]{1,2,0:T(8,128)}, u32[]{:S(2)}, u32[]{:S(2)}) collective-permute-start(f32[8,128,128]{1,2,0:T(8,128)S(1)} %get-tuple-element.7), channel_id=1, source_target_pairs={{0,64},{4,68},{8,72},{12,76},{16,80},{20,84},{24,88},{28,92},{32,9... | collective-permute-start | bytes 1572872 | tf_op jit(solution)/shard_map/ppermute | solution.py:18
  156.7 1.2 copy-start.3
  157.9 27.4 %collective-permute-start.5 = (f32[8,128,128]{1,2,0:T(8,128)}, f32[8,128,128]{1,2,0:T(8,128)S(1)}, u32[]{:S(2)}, u32[]{:S(2)}) collective-permute-start(f32[8,128,128]{1,2,0:T(8,128)} %slice_select_fusion.2), channel_id=1, source_target_pairs={{0,128},{4,132},{8,136},{12,140},{16,144},{20,148},{24,152},{28,15... | collective-permute-start | bytes 1572872 | tf_op jit(solution)/shard_map/ppermute | solution.py:18
  164.2 21.0 %copy-start.4 = (f32[8,128,256]{1,2,0:T(8,128)S(1)}, f32[8,128,256]{1,2,0:T(8,128)}, u32[]{:S(2)}) copy-start(f32[8,128,256]{1,2,0:T(8,128)} %copy-done.3) | copy-start | bytes 3145732
